TPU v7x, 32 devices: a whole 2x2x4 slice. The times are simulated.
32 devices in a mesh: tm: 4 (over y, x), height: 2 (over core), chan: 4 (over z).
Axes of the slice: x: 2, y: 2, z: 4, core: 2. Of those that a mesh axis runs over, the one named last changes fastest.
Arguments:
- features: bfloat16 [384, 8, 8, 160], P('chan', 'tm', 'height'), may hold values from -400 to 400, as said below
- cotangent: bfloat16 [384, 8, 8, 160], P('chan', 'tm', 'height'), may hold values from -6 to 6
- conv_weight: bfloat16 [384, 27, 384], P('chan'), may hold values from -0.0625 to 0.0625
- norm_gain: float32 [384], replicated, may hold values from 0.5 to 1.5
- norm_bias: float32 [384], replicated, may hold values from -3 to 3
Outputs:
- input_grad: bfloat16 [384, 8, 8, 160], P('chan', 'tm', 'height')
- weight_grad: float32 [384, 27, 384], P('chan')
Inputs may be any that keep to these rules, and one draw needn't show every extreme that they name: `features`: bounded activations.
All inputs are finite; a program needn't handle non-finite values.
Results may differ from a plain program's by a relative error of at most 0.003.
Values may be sent and summed in bfloat16 or wider, within the bound.
No kernel may reach another device: no remote copies, remote signals or barrier semaphores. Data moves between devices by JAX's collectives and lax.ppermute only.
A program may use at most 64 MiB of HBM per device.

v0:
```python
import math
import jax
import jax.numpy as jnp
from jax import lax
from jax.sharding import PartitionSpec as P


def from_behind(block, axis, distance):
    devices = range(lax.axis_size(axis))
    route = [(i - distance, i) for i in devices if i - distance in devices]
    return lax.ppermute(block, axis, route)


def with_halo(array, sides, width):
    for axis, dim in sides:
        size, length = (lax.axis_size(axis), array.shape[dim])
        up = [(i, (i + 1) % size) for i in range(size - 1)]
        down = [(j, i) for i, j in up]
        last = lax.slice_in_dim(array, length - width, length, axis=dim)
        first = lax.slice_in_dim(array, 0, width, axis=dim)
        before = lax.ppermute(last, axis, up)
        after = lax.ppermute(first, axis, down)
        array = jnp.concatenate([before, array, after], axis=dim)
    return array


def on_device(features, cotangent, conv_weight, norm_gain, norm_bias):
    chans, frames, rows, cols = features.shape
    whole_x = lax.all_gather(features, "chan", axis=0, tiled=True)
    total = whole_x.shape[0]
    flat_x = whole_x.reshape(total, -1).astype(jnp.float32)
    inv_rms = lax.rsqrt(jnp.mean(flat_x * flat_x, axis=0, keepdims=True) + 1e-06)
    normed = flat_x * inv_rms * norm_gain[:, None] + norm_bias[:, None]
    active = jax.nn.silu(normed).astype(jnp.bfloat16)
    ahead = from_behind(cotangent, "tm", -1)
    longer = jnp.concatenate([cotangent, ahead], axis=1)
    bordered = with_halo(longer, (("height", 2),), 1)
    padded = jnp.pad(bordered, ((0, 0), (0, 0), (0, 0), (1, 1)))
    taps = []
    for kt in range(3):
        for kh in range(3):
            for kw in range(3):
                taps.append(
                    padded[
                        :, 2 - kt : 2 - kt + frames, 2 - kh : 2 - kh + rows, 2 - kw : 2 - kw + cols
                    ]
                )
    stacked = jnp.stack(taps, axis=1).reshape(chans * 27, -1)
    local_sums = lax.dot_general(
        stacked, active, (((1,), (1,)), ((), ())), preferred_element_type=jnp.float32
    )
    positions = frames * lax.axis_size("tm") * rows * lax.axis_size("height") * cols
    summed = lax.psum(local_sums, ("tm", "height"))
    weight_grad = (summed / math.sqrt(positions)).reshape(chans, 27, total)
    sig = jax.nn.sigmoid(normed)
    slope = sig * (1.0 + normed * (1.0 - sig))
    offset = lax.axis_index("chan") * chans
    weight_part = conv_weight.reshape(chans * 27, chans * lax.axis_size("chan"))
    act_grad = lax.psum_scatter(
        lax.dot_general(
            weight_part, stacked, (((0,), (0,)), ((), ())), preferred_element_type=jnp.float32
        ),
        "chan",
        scatter_dimension=0,
        tiled=True,
    )
    own_x = features.reshape(chans, -1).astype(jnp.float32)
    own_slope = lax.dynamic_slice_in_dim(slope, offset, chans, 0)
    own_gain = lax.dynamic_slice_in_dim(norm_gain, offset, chans, 0)
    upstream = act_grad * own_slope * own_gain[:, None]
    dots = lax.psum(jnp.sum(upstream * own_x, axis=0, keepdims=True), "chan")
    own_back = inv_rms * upstream - own_x * inv_rms**3 * dots / total
    result = cotangent.reshape(chans, -1).astype(jnp.float32) + own_back
    return (result.astype(jnp.bfloat16).reshape(features.shape), weight_grad)


def solution(mesh):
    return jax.shard_map(
        on_device,
        mesh=mesh,
        in_specs=(
            P("chan", "tm", "height", None),
            P("chan", "tm", "height", None),
            P("chan", None, None),
            P(),
            P(),
        ),
        out_specs=(P("chan", "tm", "height", None), P("chan", None, None)),
        check_vma=False,
    )
```

profile of v0, /device:TPU:0, one launch (start us, length us, event | category | flops | bytes accessed | tf_op | source)
XLA Modules:
  0.0 245.2 jit_solution(13448478375143645336)
XLA Ops:
  8.0 1.3 collective-permute-start
  9.3 1.3 copy.16
  10.7 31.4 %all_gather.3 = bf16[384,2,4,160]{3,2,1,0:T(4,128)(2,1)S(1)} all-gather(bf16[96,2,4,160]{3,2,1,0:T(4,128)(2,1)S(1)} %copy.16), channel_id=1, replica_groups=mesh['tm'=4,'height'=2,'chan'=4] {'chan'}, dimensions={0}, use_global_device_ids=true | all-gather | bytes 1228800 | tf_op jit(solution)/shard_map/all_gather | solution.py:29
  42.1 1.4 copy.17
  43.9 1.0 constant_dynamic-update-slice_fusion.1
  45.0 1.3 collective-permute-start.1
  46.3 1.3 collective-permute-start.2
  47.6 1.4 multiply_convert_fusion
  50.0 0.8 fusion.53
  52.4 0.8 fusion.51
  54.7 0.8 fusion.49
  55.5 0.8 fusion.24
  59.5 0.8 fusion.45
  61.8 0.8 fusion.42
  64.2 0.8 fusion.40
  68.9 0.8 fusion.34
  71.3 21.1 %copy.18 = bf16[96,27,2,4,160]{4,3,2,1,0:T(4,128)(2,1)} copy(bf16[96,27,2,4,160]{0,4,3,2,1:T(8,128)(2,1)} %fusion.31) | data formatting | bytes 13271040 | tf_op jit(solution)/shard_map/stack | solution.py:48
  92.5 20.4 %reshape.67 = bf16[2592,1280]{1,0:T(8,128)(2,1)} reshape(bf16[96,27,2,4,160]{4,3,2,1,0:T(4,128)(2,1)} %copy.18) | data formatting | bytes 13271040 | tf_op jit(solution)/shard_map/reshape | solution.py:48
  112.8 8.4 %fusion.56 = f32[2592,384]{1,0:T(8,128)} fusion(bf16[2592,1280]{1,0:T(8,128)(2,1)} %reshape.67, bf16[384,1280]{0,1:T(8,128)(2,1)S(1)} %bitcast.128), kind=kOutput, calls=%fused_computation.102 | convolution fusion | flops 2548039680 | bytes 11599872 | tf_op jit(solution)/shard_map/dot_general | solution.py:49
  121.5 2.3 copy.19
  123.8 2.2 reshape.68
  126.0 6.7 %convolution_bitcast_fusion = f32[384,1280]{0,1:T(8,128)S(1)} fusion(bf16[2592,1280]{1,0:T(8,128)(2,1)} %reshape.67, bf16[2592,384]{1,0:T(8,128)(2,1)} %reshape.68), kind=kOutput, calls=%fused_computation.2 | convolution fusion | flops 2548039680 | bytes 10592256 | tf_op jit(solution)/shard_map/dot_general | solution.py:60
  132.7 1.8 copy.21
  134.7 1.8 negate_exponential_fusion
  136.5 66.4 %all-reduce.3.cloned.1.call-done = f32[2592,384]{1,0:T(8,128)} async-done(((f32[2592,384]{1,0:T(8,128)}), f32[2592,384]{1,0:T(8,128)}) %all-reduce.3.cloned.1.call-update) | async-done | bytes 3981328 | tf_op jit(solution)/shard_map/psum | solution.py:53
  202.9 4.4 %broadcast_multiply_fusion = f32[2592,384]{1,0:T(8,128)} fusion(f32[2592,384]{1,0:T(8,128)} %all-reduce.3.cloned.1.call-done), kind=kLoop, calls=%fused_computation.4 | loop fusion | flops 995328 | bytes 7962624 | tf_op jit(solution)/shard_map/div | solution.py:54
  207.3 5.0 %reshape.70 = f32[96,27,384]{2,1,0:T(8,128)} reshape(f32[2592,384]{1,0:T(8,128)} %broadcast_multiply_fusion) | data formatting | bytes 7962624 | tf_op jit(solution)/shard_map/reshape | solution.py:54
  212.3 6.6 %copy.20 = f32[96,27,384]{2,0,1:T(8,128)} copy(f32[96,27,384]{2,1,0:T(8,128)} %reshape.70) | data formatting | bytes 7962624
  218.8 2.1 copy.22
  221.0 2.8 %fusion.13 = (f32[1280]{0:T(1024)S(1)}, f32[96,1280]{0,1:T(8,128)}) fusion(bf16[96,2,4,160]{0,3,2,1:T(8,128)(2,1)S(1)} %copy-done.2, f32[96]{0:T(128)S(1)} %dynamic_slice.7, f32[96,1280]{0,1:T(8,128)} %copy.22, f32[384,1280]{0,1:T(8,128)} %get-tuple-element.13, s32[]{:T(128)S(6)} %select_n.4, f32[384,1280]{0,1:T(8,128)S(1)} %get-tuple-element.12), kind=kLoop, calls=%fused_computation.31 | loop fusion | flops 1350400 | bytes 2217348 | tf_op jit(solution)/shard_map/reduce_sum | solution.py:71
  223.8 11.6 %psum.14 = f32[1280]{0:T(1024)S(1)} all-reduce(f32[1280]{0:T(1024)S(1)} %get-tuple-element.10), channel_id=1, replica_groups=mesh['tm'=4,'height'=2,'chan'=4] {'chan'}, use_global_device_ids=true, to_apply=%region_3.4 | all-reduce | flops 1280 | bytes 10240 | tf_op jit(solution)/shard_map/psum | solution.py:71
  235.4 2.4 fusion.12
  (45 shorter events, 16.5 us)
Async XLA Ops:
  8.0 194.9 %all-reduce.3.cloned.1.call-start = ((), (), s32[]{:S(2)}) async-start(), calls=%async_computation.1 | async-start | bytes 7962624 | tf_op jit(solution)/shard_map/psum | solution.py:53
  8.0 36.9 %collective-permute-start = (bf16[96,2,4,160]{0,3,2,1:T(8,128)(2,1)}, bf16[96,2,4,160]{0,3,2,1:T(8,128)(2,1)S(1)}, u32[]{:S(2)}, u32[]{:S(2)}) collective-permute-start(bf16[96,2,4,160]{0,3,2,1:T(8,128)(2,1)} %param.6), channel_id=1, source_target_pairs={{8,0},{16,8},{24,16},{9,1},{17,9},{25,17},{10,2},{18,10},{26,18},{... | collective-permute-start | bytes 737288 | tf_op jit(solution)/shard_map/ppermute | solution.py:11
  45.0 4.0 %collective-permute-start.1 = (bf16[96,4,1,160]{0,3,2,1:T(8,128)(2,1)S(1)}, bf16[96,4,1,160]{0,3,2,1:T(8,128)(2,1)S(1)}, u32[]{:S(2)}, u32[]{:S(2)}) collective-permute-start(bf16[96,4,1,160]{0,3,2,1:T(8,128)(2,1)S(1)} %get-tuple-element.14), channel_id=1, source_target_pairs={{0,4},{1,5},{2,6},{3,7},{8,12},{9,13},{10,14},{11,15},{16,20},{17,... | collective-permute-start | bytes 368648 | tf_op jit(solution)/shard_map/ppermute | solution.py:21
  46.3 3.3 %collective-permute-start.2 = (bf16[96,4,1,160]{0,3,2,1:T(8,128)(2,1)S(1)}, bf16[96,4,1,160]{0,3,2,1:T(8,128)(2,1)S(1)}, u32[]{:S(2)}, u32[]{:S(2)}) collective-permute-start(bf16[96,4,1,160]{0,3,2,1:T(8,128)(2,1)S(1)} %get-tuple-element.15), channel_id=1, source_target_pairs={{4,0},{5,1},{6,2},{7,3},{12,8},{13,9},{14,10},{15,11},{20,16},{21,... | collective-permute-start | bytes 368648 | tf_op jit(solution)/shard_map/ppermute | solution.py:22
  50.0 17.4 %copy-start = (bf16[96,2,4,160]{0,3,2,1:T(8,128)(2,1)S(1)}, bf16[96,2,4,160]{0,3,2,1:T(8,128)(2,1)}, u32[]{:S(2)}) copy-start(bf16[96,2,4,160]{0,3,2,1:T(8,128)(2,1)} %param.6) | copy-start | bytes 737284
  121.3 97.5 %reduce-scatter.4.cloned.1.call-start = ((), (), s32[]{:S(2)}) async-start(), calls=%async_computation.2 | async-start | bytes 2457600
  126.0 8.6 %copy-start.3 = (f32[384]{0:T(512)S(1)}, f32[384]{0:T(512)}, u32[]{:S(2)}) copy-start(f32[384]{0:T(512)} %param.8) | copy-start | bytes 4612
  126.0 8.7 %copy-start.4 = (f32[384]{0:T(512)S(1)}, f32[384]{0:T(512)}, u32[]{:S(2)}) copy-start(f32[384]{0:T(512)} %param.9) | copy-start | bytes 4612
  207.3 13.7 %copy-start.2 = (bf16[96,2,4,160]{0,3,2,1:T(8,128)(2,1)S(1)}, bf16[96,2,4,160]{0,3,2,1:T(8,128)(2,1)}, u32[]{:S(2)}) copy-start(bf16[96,2,4,160]{0,3,2,1:T(8,128)(2,1)} %param.5) | copy-start | bytes 737284
  207.3 28.1 %copy-start.1 = (bf16[96,2,4,160]{0,3,2,1:T(8,128)(2,1)S(1)}, bf16[96,2,4,160]{0,3,2,1:T(8,128)(2,1)}, u32[]{:S(2)}) copy-start(bf16[96,2,4,160]{0,3,2,1:T(8,128)(2,1)} %param.6) | copy-start | bytes 737284
Sparse Core Ops, SparseCore 0:
  121.4 81.3 all-reduce.2
Sparse Core Ops, SparseCore 1:
  134.6 44.6 reduce-scatter.3
where the time goes:
time: 247 us; the launch traced here: 245 us
  local copies, waits for them, and re-layouts  82 us (33%)
  waiting for transfers between devices  67 us (27%)
  blocking collectives  43 us (17%)
  other arithmetic  18.3 us (7%)
  between operations  15.6 us (6%)
  matrix products  15.1 us (6%)
  starting transfers between devices  4.15 us (2%)
    psum x1, waiting for transfers between devices, on_device(): summed = lax.psum(local_sums, ('tm', 'height'))  66.4 us
    all_gather x1, blocking collectives, on_device(): whole_x = lax.all_gather(features, 'chan', axis=0, tiled=True)  31.4 us
    unnamed x36, local copies, waits for them, and re-layouts  30.9 us
    another operation x2, local copies, waits for them, and re-layouts, on_device(): stacked = jnp.stack(taps, axis=1).reshape(chans * 27, -1)  21.9 us
    reshape x1, local copies, waits for them, and re-layouts, on_device(): stacked = jnp.stack(taps, axis=1).reshape(chans * 27, -1)  20.4 us
    psum x1, blocking collectives, on_device(): dots = lax.psum(jnp.sum(upstream * own_x, axis=0, keepdims=True), 'chan')  11.6 us
    dot_general x1, matrix products, on_device(): lax.dot_general(stacked, active, (((1,), (1,)), ((), ())), preferred_elem...  8.42 us
    dot_general x1, matrix products, on_device(): lax.dot_general(weight_part, stacked, (((0,), (0,)), ((), ())), preferred...  6.67 us
  transfers between devices with their start and end apart: 5, of which 2 were waited for; matrix products, arithmetic and copies ran while one was open for 15% of the time, Pallas kernels for 0%

commit v1 on v0

--- a/solution.py
+++ b/solution.py
@@ -26,7 +26,23 @@
 
 def on_device(features, cotangent, conv_weight, norm_gain, norm_bias):
     chans, frames, rows, cols = features.shape
-    whole_x = lax.all_gather(features, "chan", axis=0, tiled=True)
+    ways, here, turn = (lax.axis_size("chan"), lax.axis_index("chan"), features.shape[0])
+    shape = [n * ways if d == 0 else n for d, n in enumerate(features.shape)]
+    full = lax.dynamic_update_slice_in_dim(
+        jnp.zeros(shape, features.dtype), features, here * turn, axis=0
+    )
+    going_up = going_down = features
+    for far in range(1, ways // 2 + 1):
+        going_up = lax.ppermute(going_up, "chan", [(d, (d + 1) % ways) for d in range(ways)])
+        full = lax.dynamic_update_slice_in_dim(full, going_up, (here - far) % ways * turn, axis=0)
+        if 2 * far < ways:
+            going_down = lax.ppermute(
+                going_down, "chan", [(d, (d - 1) % ways) for d in range(ways)]
+            )
+            full = lax.dynamic_update_slice_in_dim(
+                full, going_down, (here + far) % ways * turn, axis=0
+            )
+    whole_x = full
     total = whole_x.shape[0]
     flat_x = whole_x.reshape(total, -1).astype(jnp.float32)
     inv_rms = lax.rsqrt(jnp.mean(flat_x * flat_x, axis=0, keepdims=True) + 1e-06)

time: 247 us -> 231 us (0.935)
  blocking collectives: 43 us -> 11.4 us
  local copies, waits for them, and re-layouts: 82 us -> 95.5 us
  starting transfers between devices: 4.15 us -> 12.5 us
  waiting for transfers between devices: 67 us -> 60.6 us
    all_gather x1 -> x0, blocking collectives: 31.4 us -> none  [on_device(): whole_x = lax.all_gather(features, 'chan', axis=0, tiled=True)]
    dynamic_update_slice x0 -> x4, local copies, waits for them, and re-layouts: none -> 11.9 us  [the longest x2 5.98 us: on_device(): lax.dynamic_update_slice_in_dim(full, going_up, (here - far) % ways * tur...]
    psum x1, waiting for transfers between devices: 66.4 us -> 55.3 us  [on_device(): summed = lax.psum(local_sums, ('tm', 'height'))]
    ppermute x0 -> x3, starting transfers between devices: none -> 8.33 us  [the longest x2 6.24 us: on_device(): lax.ppermute(going_up, 'chan', [(d, (d + 1) % ways) for d in range(ways)])]
    ppermute x1, waiting for transfers between devices: 0.01 us -> 5.29 us  [from_behind(): return lax.ppermute(block, axis, route)]
    unnamed x36 -> x33, local copies, waits for them, and re-layouts: 30.9 us -> 31.1 us
  transfers between devices with their start and end apart: 5 -> 8, of which waited for: 2 -> 2; matrix products, arithmetic and copies ran while one was open for 15% -> 49% of each run, Pallas kernels for 0% -> 0%
where the time goes in v1:
time: 231 us; the launch traced here: 230 us
  local copies, waits for them, and re-layouts  95.5 us (41%)
  waiting for transfers between devices  60.6 us (26%)
  matrix products  17.3 us (7%)
  other arithmetic  16.7 us (7%)
  between operations  15.7 us (7%)
  starting transfers between devices  12.5 us (5%)
  blocking collectives  11.4 us (5%)
    psum x1, waiting for transfers between devices, on_device(): summed = lax.psum(local_sums, ('tm', 'height'))  55.3 us
    unnamed x33, local copies, waits for them, and re-layouts  31.1 us
    another operation x2, local copies, waits for them, and re-layouts, on_device(): stacked = jnp.stack(taps, axis=1).reshape(chans * 27, -1)  21.8 us
    reshape x1, local copies, waits for them, and re-layouts, on_device(): stacked = jnp.stack(taps, axis=1).reshape(chans * 27, -1)  20.4 us
    psum x1, blocking collectives, on_device(): dots = lax.psum(jnp.sum(upstream * own_x, axis=0, keepdims=True), 'chan')  11.4 us
    dot_general x1, matrix products, on_device(): lax.dot_general(weight_part, stacked, (((0,), (0,)), ((), ())), preferred...  8.82 us
    dot_general x1, matrix products, on_device(): lax.dot_general(stacked, active, (((1,), (1,)), ((), ())), preferred_elem...  8.44 us
    ppermute x2, starting transfers between devices, on_device(): lax.ppermute(going_up, 'chan', [(d, (d + 1) % ways) for d in range(ways)])  6.24 us
  transfers between devices with their start and end apart: 8, of which 2 were waited for; matrix products, arithmetic and copies ran while one was open for 49% of the time, Pallas kernels for 0%

profile of v1, /device:TPU:0, one launch (start us, length us, event | category | flops | bytes accessed | tf_op | source)
XLA Modules:
  0.0 229.7 jit_solution(13244334050588449443)
XLA Ops:
  8.0 1.3 collective-permute-start.3
  9.3 3.1 %collective-permute-start = (bf16[96,2,4,160]{0,3,2,1:T(8,128)(2,1)}, bf16[96,2,4,160]{0,3,2,1:T(8,128)(2,1)S(1)}, u32[]{:S(2)}, u32[]{:S(2)}) collective-permute-start(bf16[96,2,4,160]{0,3,2,1:T(8,128)(2,1)} %param.5), channel_id=1, source_target_pairs={{0,1},{1,2},{2,3},{3,0},{4,5},{5,6},{6,7},{7,4},{8,9},{9,10},{10,1... | collective-permute-start | bytes 737288 | tf_op jit(solution)/shard_map/ppermute | solution.py:36
  12.4 2.1 collective-permute-start.1
  14.5 1.0 constant_dynamic-update-slice_fusion.1
  15.5 5.3 %collective-permute-done.3 = bf16[96,2,4,160]{0,3,2,1:T(8,128)(2,1)S(1)} collective-permute-done((bf16[96,2,4,160]{0,3,2,1:T(8,128)(2,1)}, bf16[96,2,4,160]{0,3,2,1:T(8,128)(2,1)S(1)}, u32[]{:S(2)}, u32[]{:S(2)}) %collective-permute-start.3) | collective-permute-done | bytes 245792 | tf_op jit(solution)/shard_map/ppermute | solution.py:11
  21.5 1.3 collective-permute-start.4
  22.8 1.3 collective-permute-start.5
  24.3 2.8 %dynamic_update_slice.12 = bf16[384,2,4,160]{0,3,2,1:T(8,128)(2,1)S(1)} dynamic-update-slice(bf16[384,2,4,160]{0,3,2,1:T(8,128)(2,1)S(1)} %broadcast_in_dim.4, bf16[96,2,4,160]{0,3,2,1:T(8,128)(2,1)} %param.5, s32[]{:T(128)S(6)} %select_n.29, s32[]{:T(128)} %constant.44.clone.1, s32[]{:T(128)} %constant.44.clone.1, s32[]{:T(128)} %constant.44.clone.1) | dynamic-update-slice | bytes 491524 | tf_op jit(solution)/shard_map/dynamic_update_slice | solution.py:31
  27.1 3.2 %collective-permute-start.2 = (bf16[96,2,4,160]{0,3,2,1:T(8,128)(2,1)S(1)}, bf16[96,2,4,160]{0,3,2,1:T(8,128)(2,1)S(1)}, u32[]{:S(2)}, u32[]{:S(2)}) collective-permute-start(bf16[96,2,4,160]{0,3,2,1:T(8,128)(2,1)S(1)} %collective-permute-done), channel_id=1, source_target_pairs={{0,1},{1,2},{2,3},{3,0},{4,5},{5,6},{6,7},{7,4},{8,9},{9,10},{10,1... | collective-permute-start | bytes 737288 | tf_op jit(solution)/shard_map/ppermute | solution.py:36
  30.2 2.9 %dynamic_update_slice.13 = bf16[384,2,4,160]{0,3,2,1:T(8,128)(2,1)S(1)} dynamic-update-slice(bf16[384,2,4,160]{0,3,2,1:T(8,128)(2,1)S(1)} %dynamic_update_slice.12, bf16[96,2,4,160]{0,3,2,1:T(8,128)(2,1)S(1)} %collective-permute-done, s32[]{:T(128)S(6)} %select_n.31, s32[]{:T(128)} %constant.44.clone.1, s32[]{:T(128)} %constant.44.clone.1, s32[]{:T(128)} %constant.44.clone.1) | dynamic-update-slice | bytes 491524 | tf_op jit(solution)/shard_map/dynamic_update_slice | solution.py:37
  33.1 3.1 %dynamic_update_slice.14 = bf16[384,2,4,160]{0,3,2,1:T(8,128)(2,1)S(1)} dynamic-update-slice(bf16[384,2,4,160]{0,3,2,1:T(8,128)(2,1)S(1)} %dynamic_update_slice.13, bf16[96,2,4,160]{0,3,2,1:T(8,128)(2,1)S(1)} %collective-permute-done.1, s32[]{:T(128)S(6)} %select_n.33, s32[]{:T(128)} %constant.44.clone.1, s32[]{:T(128)} %constant.44.clone.1, s32[]{:T(128)} %constant.44.clone.1) | dynamic-update-slice | bytes 491524 | tf_op jit(solution)/shard_map/dynamic_update_slice | solution.py:42
  36.7 0.8 fusion.53
  48.4 0.8 fusion.42
  50.8 0.8 fusion.40
  55.5 0.8 fusion.34
  57.9 21.1 %copy.11 = bf16[96,27,2,4,160]{4,3,2,1,0:T(4,128)(2,1)} copy(bf16[96,27,2,4,160]{0,4,3,2,1:T(8,128)(2,1)} %fusion.31) | data formatting | bytes 13271040 | tf_op jit(solution)/shard_map/stack | solution.py:64
  78.9 20.4 %reshape.67 = bf16[2592,1280]{1,0:T(8,128)(2,1)} reshape(bf16[96,27,2,4,160]{4,3,2,1,0:T(4,128)(2,1)} %copy.11) | data formatting | bytes 13271040 | tf_op jit(solution)/shard_map/reshape | solution.py:64
  99.4 3.1 %dynamic_update_slice.15 = bf16[384,2,4,160]{0,3,2,1:T(8,128)(2,1)S(1)} dynamic-update-slice(bf16[384,2,4,160]{0,3,2,1:T(8,128)(2,1)S(1)} %dynamic_update_slice.14, bf16[96,2,4,160]{0,3,2,1:T(8,128)(2,1)S(1)} %collective-permute-done.2, s32[]{:T(128)S(6)} %select_n.35, s32[]{:T(128)} %constant.44.clone.1, s32[]{:T(128)} %constant.44.clone.1, s32[]{:T(128)} %constant.44.clone.1) | dynamic-update-slice | bytes 491524 | tf_op jit(solution)/shard_map/dynamic_update_slice | solution.py:37
  103.6 8.4 %fusion.56 = f32[2592,384]{1,0:T(8,128)} fusion(bf16[2592,1280]{1,0:T(8,128)(2,1)} %reshape.67, bf16[384,1280]{0,1:T(8,128)(2,1)S(1)} %bitcast.128), kind=kOutput, calls=%fused_computation.102 | convolution fusion | flops 2548039680 | bytes 11599872 | tf_op jit(solution)/shard_map/dot_general | solution.py:65
  112.3 3.7 %copy.12 = bf16[96,27,384]{2,1,0:T(8,128)(2,1)} copy(bf16[96,27,384]{2,0,1:T(8,128)(2,1)} %param.7) | data formatting | bytes 3981312 | tf_op args[2]
  116.0 4.3 %reshape.68 = bf16[2592,384]{1,0:T(8,128)(2,1)} reshape(bf16[96,27,384]{2,1,0:T(8,128)(2,1)} %copy.12) | data formatting | bytes 3981312 | tf_op jit(solution)/shard_map/reshape | solution.py:74
  120.3 8.8 %convolution_bitcast_fusion = f32[384,1280]{0,1:T(8,128)} fusion(bf16[2592,1280]{1,0:T(8,128)(2,1)} %reshape.67, bf16[2592,384]{1,0:T(8,128)(2,1)} %reshape.68), kind=kOutput, calls=%fused_computation.2 | convolution fusion | flops 2548039680 | bytes 10592256 | tf_op jit(solution)/shard_map/dot_general | solution.py:76
  129.1 2.9 %copy.14 = f32[384,1280]{1,0:T(8,128)} copy(f32[384,1280]{0,1:T(8,128)} %convolution_bitcast_fusion) | data formatting | bytes 3932160
  132.2 2.4 %negate_exponential_fusion = (f32[384,1280]{0,1:T(8,128)}, f32[384,1280]{0,1:T(8,128)}) fusion(f32[384]{0:T(512)S(1)} %copy-done.3, f32[384]{0:T(512)S(1)} %copy-done.2, f32[1280]{0:T(1024)S(1)} %rsqrt.16, bf16[384,2,4,160]{0,3,2,1:T(8,128)(2,1)S(1)} %dynamic_update_slice.15), kind=kLoop, calls=%fused_computation.9 | loop fusion | flops 2457600 | bytes 4923392 | tf_op jit(solution)/shard_map/exp | solution.py:71
  134.7 55.3 %all-reduce.3.cloned.1.call-done = f32[2592,384]{1,0:T(8,128)} async-done(((f32[2592,384]{1,0:T(8,128)}), f32[2592,384]{1,0:T(8,128)}) %all-reduce.3.cloned.1.call-update) | async-done | bytes 3981328 | tf_op jit(solution)/shard_map/psum | solution.py:69
  189.9 4.4 %broadcast_multiply_fusion = f32[2592,384]{1,0:T(8,128)} fusion(f32[2592,384]{1,0:T(8,128)} %all-reduce.3.cloned.1.call-done), kind=kLoop, calls=%fused_computation.4 | loop fusion | flops 995328 | bytes 7962624 | tf_op jit(solution)/shard_map/div | solution.py:70
  194.3 5.0 %reshape.70 = f32[96,27,384]{2,1,0:T(8,128)} reshape(f32[2592,384]{1,0:T(8,128)} %broadcast_multiply_fusion) | data formatting | bytes 7962624 | tf_op jit(solution)/shard_map/reshape | solution.py:70
  199.3 6.6 %copy.13 = f32[96,27,384]{2,0,1:T(8,128)} copy(f32[96,27,384]{2,1,0:T(8,128)} %reshape.70) | data formatting | bytes 7962624
  205.9 1.3 copy.15
  207.2 2.3 %fusion.13 = (f32[1280]{0:T(1024)S(1)}, f32[96,1280]{0,1:T(8,128)S(1)}) fusion(bf16[96,2,4,160]{0,3,2,1:T(8,128)(2,1)S(1)} %copy-done.1, f32[96]{0:T(128)S(1)} %dynamic_slice.7, f32[96,1280]{0,1:T(8,128)S(1)} %copy.15, f32[384,1280]{0,1:T(8,128)} %get-tuple-element.11, s32[]{:T(128)S(6)} %select_n.29, f32[384,1280]{0,1:T(8,128)} %get-tuple-element.10), kind=kLoop, calls=%fused_computation.31 | loop fusion | flops 1350400 | bytes 2217348 | tf_op jit(solution)/shard_map/reduce_sum | solution.py:87
  209.5 11.4 %psum.14 = f32[1280]{0:T(1024)S(1)} all-reduce(f32[1280]{0:T(1024)S(1)} %get-tuple-element.8), channel_id=1, replica_groups=mesh['tm'=4,'height'=2,'chan'=4] {'chan'}, use_global_device_ids=true, to_apply=%region_3.4 | all-reduce | flops 1280 | bytes 10240 | tf_op jit(solution)/shard_map/psum | solution.py:87
  220.9 1.3 fusion.12
  (51 shorter events, 20.6 us)
Async XLA Ops:
  8.0 181.9 %all-reduce.3.cloned.1.call-start = ((), (), s32[]{:S(2)}) async-start(), calls=%async_computation.1 | async-start | bytes 7962624 | tf_op jit(solution)/shard_map/psum | solution.py:69
  8.0 12.8 %collective-permute-start.3 = (bf16[96,2,4,160]{0,3,2,1:T(8,128)(2,1)}, bf16[96,2,4,160]{0,3,2,1:T(8,128)(2,1)S(1)}, u32[]{:S(2)}, u32[]{:S(2)}) collective-permute-start(bf16[96,2,4,160]{0,3,2,1:T(8,128)(2,1)} %param.6), channel_id=1, source_target_pairs={{8,0},{16,8},{24,16},{9,1},{17,9},{25,17},{10,2},{18,10},{26,18},{... | collective-permute-start | bytes 737288 | tf_op jit(solution)/shard_map/ppermute | solution.py:11
  9.3 17.7 %collective-permute-start = (bf16[96,2,4,160]{0,3,2,1:T(8,128)(2,1)}, bf16[96,2,4,160]{0,3,2,1:T(8,128)(2,1)S(1)}, u32[]{:S(2)}, u32[]{:S(2)}) collective-permute-start(bf16[96,2,4,160]{0,3,2,1:T(8,128)(2,1)} %param.5), channel_id=1, source_target_pairs={{0,1},{1,2},{2,3},{3,0},{4,5},{5,6},{6,7},{7,4},{8,9},{9,10},{10,1... | collective-permute-start | bytes 737288 | tf_op jit(solution)/shard_map/ppermute | solution.py:36
  12.4 20.7 %collective-permute-start.1 = (bf16[96,2,4,160]{0,3,2,1:T(8,128)(2,1)}, bf16[96,2,4,160]{0,3,2,1:T(8,128)(2,1)S(1)}, u32[]{:S(2)}, u32[]{:S(2)}) collective-permute-start(bf16[96,2,4,160]{0,3,2,1:T(8,128)(2,1)} %param.5), channel_id=1, source_target_pairs={{0,3},{1,0},{2,1},{3,2},{4,7},{5,4},{6,5},{7,6},{8,11},{9,8},{10,9... | collective-permute-start | bytes 737288 | tf_op jit(solution)/shard_map/ppermute | solution.py:39
  21.5 14.7 %collective-permute-start.4 = (bf16[96,4,1,160]{0,3,2,1:T(8,128)(2,1)}, bf16[96,4,1,160]{0,3,2,1:T(8,128)(2,1)S(1)}, u32[]{:S(2)}, u32[]{:S(2)}) collective-permute-start(bf16[96,4,1,160]{0,3,2,1:T(8,128)(2,1)} %get-tuple-element.12), channel_id=1, source_target_pairs={{0,4},{1,5},{2,6},{3,7},{8,12},{9,13},{10,14},{11,15},{16,20},{17,... | collective-permute-start | bytes 368648 | tf_op jit(solution)/shard_map/ppermute | solution.py:21
  22.8 13.5 %collective-permute-start.5 = (bf16[96,4,1,160]{0,3,2,1:T(8,128)(2,1)S(1)}, bf16[96,4,1,160]{0,3,2,1:T(8,128)(2,1)S(1)}, u32[]{:S(2)}, u32[]{:S(2)}) collective-permute-start(bf16[96,4,1,160]{0,3,2,1:T(8,128)(2,1)S(1)} %get-tuple-element.13), channel_id=1, source_target_pairs={{4,0},{5,1},{6,2},{7,3},{12,8},{13,9},{14,10},{15,11},{20,16},{21,... | collective-permute-start | bytes 368648 | tf_op jit(solution)/shard_map/ppermute | solution.py:22
  27.1 72.3 %collective-permute-start.2 = (bf16[96,2,4,160]{0,3,2,1:T(8,128)(2,1)S(1)}, bf16[96,2,4,160]{0,3,2,1:T(8,128)(2,1)S(1)}, u32[]{:S(2)}, u32[]{:S(2)}) collective-permute-start(bf16[96,2,4,160]{0,3,2,1:T(8,128)(2,1)S(1)} %collective-permute-done), channel_id=1, source_target_pairs={{0,1},{1,2},{2,3},{3,0},{4,5},{5,6},{6,7},{7,4},{8,9},{9,10},{10,1... | collective-permute-start | bytes 737288 | tf_op jit(solution)/shard_map/ppermute | solution.py:36
  36.7 17.3 %copy-start = (bf16[96,2,4,160]{0,3,2,1:T(8,128)(2,1)S(1)}, bf16[96,2,4,160]{0,3,2,1:T(8,128)(2,1)}, u32[]{:S(2)}) copy-start(bf16[96,2,4,160]{0,3,2,1:T(8,128)(2,1)} %param.6) | copy-start | bytes 737284
  78.9 23.9 %copy-start.2 = (f32[384]{0:T(512)S(1)}, f32[384]{0:T(512)}, u32[]{:S(2)}) copy-start(f32[384]{0:T(512)} %param.8) | copy-start | bytes 4612
  78.9 23.9 %copy-start.3 = (f32[384]{0:T(512)S(1)}, f32[384]{0:T(512)}, u32[]{:S(2)}) copy-start(f32[384]{0:T(512)} %param.9) | copy-start | bytes 4612
  112.0 93.8 %reduce-scatter.4.cloned.1.call-start = ((), (), s32[]{:S(2)}) async-start(), calls=%async_computation.2 | async-start | bytes 2457600
  194.3 12.8 %copy-start.1 = (bf16[96,2,4,160]{0,3,2,1:T(8,128)(2,1)S(1)}, bf16[96,2,4,160]{0,3,2,1:T(8,128)(2,1)}, u32[]{:S(2)}) copy-start(bf16[96,2,4,160]{0,3,2,1:T(8,128)(2,1)} %param.5) | copy-start | bytes 737284
Sparse Core Ops, SparseCore 0:
  112.2 77.7 all-reduce.2
Sparse Core Ops, SparseCore 1:
  132.2 40.2 reduce-scatter.3
